TPU v7x, 512 devices: a whole 4x8x8 slice. The times are simulated.
512 devices in a mesh: dp: 32 (over x, z), mp: 16 (over y, core).
Axes of the slice: x: 4, y: 8, z: 8, core: 2. Of those that a mesh axis runs over, the one named last changes fastest.
Arguments:
- hidden_rows: bfloat16 [16384, 8192], P('dp', 'mp'), may hold values from -6 to 6
- base_weight: bfloat16 [8192, 4096], P('mp'), may hold values from -0.0625 to 0.0625
- adapter_down: bfloat16 [32, 64, 8192], P('dp', None, 'mp'), may hold values from -0.0625 to 0.0625
- adapter_up: bfloat16 [32, 64, 4096], P('dp', None, 'mp'), may hold values from -0.75 to 0.75
- adapter_of_row: int32 [16384, 1], P('dp'), may hold values from 0 to 31; in each aligned block of 512 rows (0 to 511, 512 to 1023, ...) at most 32 rows name the same one
- holder_map: int32 [32], replicated, may hold values from 0 to 31, each once
Outputs:
- projected: bfloat16 [16384, 4096], P('dp', 'mp')
Inputs may be any that keep to these rules, and one draw needn't show every extreme that they name: `adapter_of_row`: within the 512 rows of one index of dp (aligned blocks), no adapter is named by more than 32 rows; every adapter is named by some row. `holder_map`: each of the 32 slots holds exactly one adapter.
All inputs are finite; a program needn't handle non-finite values.
Results may differ from a plain program's by a relative error of at most 0.02.
Values may be sent and summed in bfloat16 or wider, within the bound.
No kernel may reach another device: no remote copies, remote signals or barrier semaphores. Data moves between devices by JAX's collectives and lax.ppermute only.
A program may use at most 64 MiB of HBM per device.

v0:
```python
import jax
import jax.numpy as jnp
from jax import lax
from jax.sharding import PartitionSpec as P


def per_device(hidden_rows, base_weight, adapter_down, adapter_up, adapter_of_row, holder_map):
    row_count, feat_width = hidden_rows.shape
    holders = lax.axis_size("dp")
    capacity = 2 * row_count // holders
    adapter_ids = adapter_of_row[:, 0]
    matches = adapter_ids[:, None] == jnp.arange(holder_map.shape[0], dtype=jnp.int32)[None, :]
    slot_of_row = jnp.sum(jnp.where(matches, holder_map[None, :], 0), axis=1)
    members = (slot_of_row[:, None] == jnp.arange(holders, dtype=jnp.int32)[None, :]).astype(
        jnp.int32
    )
    earlier = jnp.cumsum(members, axis=0) - members
    position = jnp.sum(earlier * members, axis=1)
    destination = slot_of_row * capacity + position
    packed = (
        jnp.zeros((holders * capacity, feat_width), jnp.bfloat16).at[destination].set(hidden_rows)
    )
    packed = packed.reshape(holders, capacity, feat_width)
    base_terms = jnp.dot(hidden_rows, base_weight, preferred_element_type=jnp.float32)
    base_total = lax.psum_scatter(
        base_terms.astype(jnp.bfloat16), "mp", scatter_dimension=1, tiled=True
    ).astype(jnp.float32)
    section = packed
    partial_value = jnp.einsum(
        "hcf,hkf->hck",
        section,
        lax.all_gather(adapter_down, "dp", axis=0, tiled=True),
        preferred_element_type=jnp.float32,
    )
    reduced = lax.psum(partial_value.astype(jnp.bfloat16), "mp")
    section = reduced
    buckets = jnp.einsum(
        "hck,hko->hco",
        section,
        lax.all_gather(adapter_up, "dp", axis=0, tiled=True),
        preferred_element_type=jnp.float32,
    ).astype(jnp.bfloat16)
    adapter_out = buckets.reshape(holders * capacity, buckets.shape[2])[destination]
    return (base_total + adapter_out.astype(jnp.float32)).astype(jnp.bfloat16)


def solution(mesh):
    placed = (
        P("dp", "mp"),
        P("mp", None),
        P("dp", None, "mp"),
        P("dp", None, "mp"),
        P("dp", None),
        P(),
    )
    return jax.shard_map(
        per_device, mesh=mesh, in_specs=placed, out_specs=P("dp", "mp"), check_vma=False
    )
```

profile of v0, /device:TPU:27, one launch (start us, length us, event | category | flops | bytes accessed | tf_op | source)
XLA Modules:
  0.0 372.1 jit_solution(2252982581453105532)
XLA Ops:
  6.5 0.0 copy-start
  6.5 0.0 all-gather.3.cloned.1.call-start
  6.5 0.7 all-gather.3.cloned.1.call-update
  7.3 0.0 all-gather.5.cloned.1.call-start
  7.3 0.7 all-gather.5.cloned.1.call-update
  8.0 0.0 all-reduce.2.cloned.1.call-start
  8.1 0.8 select_reduce_fusion
  8.9 1.2 reduce-window.6
  10.0 0.2 slice_reduce_fusion
  10.3 0.1 fusion.4
  10.4 3.2 scatter_custom_fusion
  13.6 80.2 %all-gather.3.cloned.1.call-done = bf16[32,64,512]{2,1,0:T(8,128)(2,1)} async-done(((bf16[1,64,512]{2,1,0:T(8,128)(2,1)}), bf16[32,64,512]{2,1,0:T(8,128)(2,1)}) %all-gather.3.cloned.1.call-update) | async-done | bytes 2097168 | tf_op jit(solution)/shard_map/all_gather | solution.py:32
  93.9 3.0 convolution_convert_fusion.2
  96.9 0.0 all-reduce.2.cloned.1.call-update
  96.9 0.0 reduce-scatter.2.cloned.1.call-start
  96.9 0.0 copy-done
  96.9 6.5 %convolution_convert_fusion = bf16[512,4096]{1,0:T(8,128)(2,1)} fusion(bf16[512,512]{1,0:T(8,128)(2,1)S(1)} %copy-done, bf16[512,4096]{1,0:T(8,128)(2,1)} %param.7), kind=kOutput, calls=%fused_computation.2 | convolution fusion | flops 2149580800 | bytes 8912896 | tf_op jit(solution)/shard_map/dot_general | solution.py:24
  103.5 0.0 reduce-scatter.2.cloned.1.call-update
  103.5 72.3 %all-gather.5.cloned.1.call-done = bf16[32,64,256]{2,1,0:T(8,128)(2,1)} async-done(((bf16[1,64,256]{2,1,0:T(8,128)(2,1)}), bf16[32,64,256]{2,1,0:T(8,128)(2,1)}) %all-gather.5.cloned.1.call-update) | async-done | bytes 1048592 | tf_op jit(solution)/shard_map/all_gather | solution.py:40
  175.8 119.3 %all-reduce.2.cloned.1.call-done = bf16[32,32,64]{2,1,0:T(8,128)(2,1)} async-done(((bf16[32,32,64]{2,1,0:T(8,128)(2,1)}), bf16[32,32,64]{2,1,0:T(8,128)(2,1)}) %all-reduce.2.cloned.1.call-update) | async-done | bytes 131088 | tf_op jit(solution)/shard_map/psum | solution.py:35
  295.1 1.6 convolution_convert_fusion.1
  296.7 2.0 gather_fusion
  298.7 65.1 %reduce-scatter.2.cloned.1.call-done = bf16[512,256]{1,0:T(8,128)(2,1)} async-done(((bf16[512,4096]{1,0:T(8,128)(2,1)}), bf16[512,256]{1,0:T(8,128)(2,1)}) %reduce-scatter.2.cloned.1.call-update) | async-done | bytes 262160 | tf_op jit(solution)/shard_map/reduce_scatter | solution.py:25
  363.8 1.7 add_convert_fusion
  (6 shorter events, 0.1 us)
Async XLA Ops:
  6.5 90.4 %copy-start = (bf16[512,512]{1,0:T(8,128)(2,1)S(1)}, bf16[512,512]{1,0:T(8,128)(2,1)}, u32[]{:S(2)}) copy-start(bf16[512,512]{1,0:T(8,128)(2,1)} %param.6) | copy-start | bytes 1572868
  6.5 87.3 %all-gather.3.cloned.1.call-start = ((), (), s32[]{:S(2)}) async-start(), calls=%async_computation.2 | async-start | bytes 2162688 | tf_op jit(solution)/shard_map/all_gather | solution.py:32
  7.3 168.6 %all-gather.5.cloned.1.call-start = ((), (), s32[]{:S(2)}) async-start(), calls=%async_computation.4 | async-start | bytes 1081344 | tf_op jit(solution)/shard_map/all_gather | solution.py:40
  8.0 287.1 %all-reduce.2.cloned.1.call-start = ((), (), s32[]{:S(2)}) async-start(), calls=%async_computation.3 | async-start | bytes 524288 | tf_op jit(solution)/shard_map/psum | solution.py:35
  96.9 266.9 %reduce-scatter.2.cloned.1.call-start = ((), (), s32[]{:S(2)}) async-start(), calls=%async_computation.1 | async-start | bytes 4456448 | tf_op jit(solution)/shard_map/reduce_scatter | solution.py:25
Sparse Core Ops, SparseCore 0:
  10.5 83.2 all-gather.2
  97.1 78.7 all-gather.4
  178.2 116.8 all-reduce.1
  298.0 65.7 reduce-scatter.1
where the time goes:
time: 372 us
  waiting for transfers between devices  338 us (91%)
  between operations  13.2 us (4%)
  matrix products  11.1 us (3%)
  local copies, waits for them, and re-layouts  5.4 us (1%)
  other arithmetic  3.85 us (1%)
    psum x1, waiting for transfers between devices, per_device(): reduced = lax.psum(partial_value.astype(jnp.bfloat16), 'mp')  119 us
    all_gather x1, waiting for transfers between devices, per_device(): lax.all_gather(adapter_down, 'dp', axis=0, tiled=True)  80.2 us
    all_gather x1, waiting for transfers between devices, per_device(): lax.all_gather(adapter_up, 'dp', axis=0, tiled=True)  72.3 us
    reduce_scatter x1, waiting for transfers between devices, per_device(): lax.psum_scatter(base_terms.astype(jnp.bfloat16), 'mp', scatter_dimension...  65.1 us
  transfers between devices with their start and end apart: 4, of which 4 were waited for; matrix products, arithmetic and copies ran while one was open for 5% of the time, Pallas kernels for 0%

commit v1 on v0

--- a/solution.py
+++ b/solution.py
@@ -32,7 +32,9 @@
         lax.all_gather(adapter_down, "dp", axis=0, tiled=True),
         preferred_element_type=jnp.float32,
     )
-    reduced = lax.psum(partial_value.astype(jnp.bfloat16), "mp")
+    own = partial_value.astype(jnp.bfloat16)
+    parts = lax.all_gather(own, "mp")
+    reduced = jnp.sum(parts, axis=0)
     section = reduced
     buckets = jnp.einsum(
         "hck,hko->hco",

time: 372 us -> 302 us (0.81)
  the two profiles are of different devices: /device:TPU:27 before, /device:TPU:31 now
where the time goes in v1:
time: 302 us
  waiting for transfers between devices  265 us (88%)
  between operations  13.2 us (4%)
  matrix products  11.1 us (4%)
  other arithmetic  6.92 us (2%)
  local copies, waits for them, and re-layouts  5.4 us (2%)
    all_gather x1, waiting for transfers between devices, per_device(): lax.all_gather(adapter_down, 'dp', axis=0, tiled=True)  80.3 us
    all_gather x1, waiting for transfers between devices, per_device(): lax.all_gather(adapter_up, 'dp', axis=0, tiled=True)  75.8 us
    reduce_scatter x1, waiting for transfers between devices, per_device(): lax.psum_scatter(base_terms.astype(jnp.bfloat16), 'mp', scatter_dimension...  67.9 us
    all_gather x1, waiting for transfers between devices, per_device(): parts = lax.all_gather(own, 'mp')  39.7 us
    dot_general x1, matrix products, per_device(): jnp.dot(hidden_rows, base_weight, preferred_element_type=jnp.float32)  6.57 us
  transfers between devices with their start and end apart: 4, of which 4 were waited for; matrix products, arithmetic and copies ran while one was open for 6% of the time, Pallas kernels for 0%

profile of v1, /device:TPU:31, one launch (start us, length us, event | category | flops | bytes accessed | tf_op | source)
XLA Modules:
  0.0 301.7 jit_solution(7433611121004292582)
XLA Ops:
  6.5 0.0 all-gather.5.cloned.1.call-start
  6.5 0.7 all-gather.5.cloned.1.call-update
  7.3 0.0 all-gather.9.cloned.1.call-start
  7.3 0.8 select_reduce_fusion
  8.1 1.2 reduce-window.6
  9.3 0.2 slice_reduce_fusion
  9.5 0.1 fusion.4
  9.7 3.2 %scatter_custom_fusion = bf16[1024,512]{1,0:T(8,128)(2,1)S(1)} fusion(s32[512]{0:T(512)S(1)} %bitcast.36, bf16[512,512]{1,0:T(8,128)(2,1)} %param.6, bf16[]{:T(256)} %constant.4.clone.1), kind=kCustom, calls=%fused_computation.6 | custom fusion | bytes 1049088 | tf_op jit(solution)/shard_map/scatter | solution.py:21
  12.9 80.3 %all-gather.5.cloned.1.call-done = bf16[32,64,512]{2,1,0:T(8,128)(2,1)} async-done(((bf16[1,64,512]{2,1,0:T(8,128)(2,1)}), bf16[32,64,512]{2,1,0:T(8,128)(2,1)}) %all-gather.5.cloned.1.call-update) | async-done | bytes 2097168 | tf_op jit(solution)/shard_map/all_gather | solution.py:32
  93.2 3.0 convolution_convert_fusion.2
  96.2 0.0 all-gather.9.cloned.1.call-update
  96.2 0.0 all-gather.7.cloned.1.call-start
  96.2 0.7 all-gather.7.cloned.1.call-update
  96.9 0.0 reduce-scatter.2.cloned.1.call-start
  97.0 0.0 copy-done
  97.0 6.6 %convolution_convert_fusion = bf16[512,4096]{1,0:T(8,128)(2,1)} fusion(bf16[512,512]{1,0:T(8,128)(2,1)S(1)} %copy-done, bf16[512,4096]{1,0:T(8,128)(2,1)} %param.7), kind=kOutput, calls=%fused_computation.2 | convolution fusion | flops 2149580800 | bytes 8912896 | tf_op jit(solution)/shard_map/dot_general | solution.py:24
  103.6 0.0 reduce-scatter.2.cloned.1.call-update
  103.6 39.7 %all-gather.9.cloned.1.call-done = bf16[512,32,64]{2,1,0:T(8,128)(2,1)} async-done(((bf16[32,32,64]{2,1,0:T(8,128)(2,1)}), bf16[512,32,64]{2,1,0:T(8,128)(2,1)}) %all-gather.9.cloned.1.call-update) | async-done | bytes 2097168 | tf_op jit(solution)/shard_map/all_gather | solution.py:36
  143.3 3.1 %reduce_sum.32 = bf16[32,32,64]{2,1,0:T(8,128)(2,1)S(1)} reduce(bf16[16,32,32,64]{3,2,1,0:T(8,128)(2,1)} %bitcast.33, bf16[]{:T(256)} %constant.4.clone.1), dimensions={0}, to_apply=%region_6.7 | reduce | flops 983040 | bytes 2228226 | tf_op jit(solution)/shard_map/reduce_sum | solution.py:37
  146.4 75.8 %all-gather.7.cloned.1.call-done = bf16[32,64,256]{2,1,0:T(8,128)(2,1)} async-done(((bf16[1,64,256]{2,1,0:T(8,128)(2,1)}), bf16[32,64,256]{2,1,0:T(8,128)(2,1)}) %all-gather.7.cloned.1.call-update) | async-done | bytes 1048592 | tf_op jit(solution)/shard_map/all_gather | solution.py:42
  222.1 1.5 convolution_convert_fusion.1
  223.6 2.0 gather_fusion
  225.6 67.9 %reduce-scatter.2.cloned.1.call-done = bf16[512,256]{1,0:T(8,128)(2,1)} async-done(((bf16[512,4096]{1,0:T(8,128)(2,1)}), bf16[512,256]{1,0:T(8,128)(2,1)}) %reduce-scatter.2.cloned.1.call-update) | async-done | bytes 262160 | tf_op jit(solution)/shard_map/reduce_scatter | solution.py:25
  293.5 1.7 add_convert_fusion
  (7 shorter events, 0.1 us)
Async XLA Ops:
  6.5 90.4 %copy-start = (bf16[512,512]{1,0:T(8,128)(2,1)S(1)}, bf16[512,512]{1,0:T(8,128)(2,1)}, u32[]{:S(2)}) copy-start(bf16[512,512]{1,0:T(8,128)(2,1)} %param.6) | copy-start | bytes 1572868
  6.5 86.7 %all-gather.5.cloned.1.call-start = ((), (), s32[]{:S(2)}) async-start(), calls=%async_computation.2 | async-start | bytes 2162688 | tf_op jit(solution)/shard_map/all_gather | solution.py:32
  7.3 136.0 %all-gather.9.cloned.1.call-start = ((), (), s32[]{:S(2)}) async-start(), calls=%async_computation.4 | async-start | bytes 4456448 | tf_op jit(solution)/shard_map/all_gather | solution.py:36
  96.2 125.9 %all-gather.7.cloned.1.call-start = ((), (), s32[]{:S(2)}) async-start(), calls=%async_computation.3 | async-start | bytes 1081344 | tf_op jit(solution)/shard_map/all_gather | solution.py:42
  96.9 196.5 %reduce-scatter.2.cloned.1.call-start = ((), (), s32[]{:S(2)}) async-start(), calls=%async_computation.1 | async-start | bytes 4456448 | tf_op jit(solution)/shard_map/reduce_scatter | solution.py:25
Sparse Core Ops, SparseCore 0:
  10.5 82.6 all-gather.4
  96.3 46.9 all-gather.8
  146.5 75.5 all-gather.6
  224.8 68.6 reduce-scatter.1
